TPU v7x, 32 devices: a whole 2x2x4 slice. The times are simulated.
32 devices in a mesh: gx: 8 (over z, x), gy: 4 (over y, core).
Axes of the slice: x: 2, y: 2, z: 4, core: 2. Of those that a mesh axis runs over, the one named last changes fastest.
Arguments:
- inputs: bfloat16 [3, 256, 8192], P(None, 'gy', 'gx'), may hold values from -600 to 600
- norm_gain: bfloat16 [8192], P('gx'), may hold values from 0.099609375 to 1.8984375
- query_weight: bfloat16 [8192, 8192], P('gx', 'gy'), may hold values from -0.0625 to 0.0625
- key_weight: bfloat16 [8192, 1024], P('gx', 'gy'), may hold values from -0.0625 to 0.0625
- value_weight: bfloat16 [8192, 1024], P('gx', 'gy'), may hold values from -0.0625 to 0.0625
- output_weight: bfloat16 [8192, 8192], P('gy', 'gx'), may hold values from -0.0625 to 0.0625
- query_down: bfloat16 [256, 8192, 64], P('gy', 'gx'), may hold values from -0.0625 to 0.0625
- query_up: bfloat16 [256, 64, 8192], P('gx', None, 'gy'), may hold values from -0.75 to 0.75
- output_down: bfloat16 [256, 8192, 64], P('gx', 'gy'), may hold values from -0.0625 to 0.0625
- output_up: bfloat16 [256, 64, 8192], P('gy', None, 'gx'), may hold values from -0.75 to 0.75
- block_adapter: int32 [2], replicated, may hold values from 0 to 255
- cache_lengths: int32 [256], P(('gx', 'gy')), may hold values from 1 to 256, as said below
- cache_keys: bfloat16 [256, 256, 1024], P(('gx', 'gy')), may hold values from -160 to 160
- cache_values: bfloat16 [256, 256, 1024], P(('gx', 'gy')), may hold values from -6 to 6
Outputs:
- block_output: bfloat16 [3, 256, 8192], P(None, 'gy', 'gx')
Inputs may be any that keep to these rules, and one draw needn't show every extreme that they name: `cache_lengths`: some request has exactly 256 cached positions.
All inputs are finite; a program needn't handle non-finite values.
Results may differ from a plain program's by a relative error of at most 0.012.
The roundings to bfloat16 on the way count: a program that leaves them out, or rounds other values in their place, can miss the bound.
Values may be sent and summed in bfloat16 or wider, within the bound.
No kernel may reach another device: no remote copies, remote signals or barrier semaphores. Data moves between devices by JAX's collectives and lax.ppermute only.
A program may use at most 192 MiB of HBM per device.

v0:
```python
import jax
import jax.numpy as jnp
from jax import lax
from jax.sharding import PartitionSpec as P

QUERY_HEADS = 64
KEY_VALUE_HEADS = 8
HEAD_FEATURES = 128
BLOCK = 128
EPS = 1e-05
THETA = 500000.0


def rotary_embedding(values_in, token_positions):
    half_size = values_in.shape[-1] // 2
    exponent = jnp.arange(half_size, dtype=jnp.float32) * 2.0 / values_in.shape[-1]
    frequency = THETA ** (-exponent)
    angles = token_positions.astype(jnp.float32)[:, None] * frequency[None, :]
    cosine = jnp.cos(angles)[:, None, :]
    sine_part = jnp.sin(angles)[:, None, :]
    lower = values_in[..., :half_size]
    upper = values_in[..., half_size:]
    return jnp.concatenate(
        [lower * cosine - upper * sine_part, upper * cosine + lower * sine_part], axis=-1
    )


def pick_adapters(table, adapter_ids, owner_index):
    table_count = table.shape[0]
    picked = []
    for block in range(adapter_ids.shape[0]):
        wanted = adapter_ids[block]
        owned = wanted // table_count == owner_index
        entry = lax.dynamic_index_in_dim(table, wanted % table_count, axis=0, keepdims=False)
        picked.append(jnp.where(owned, entry, jnp.zeros_like(entry)))
    return jnp.stack(picked)


def attend(query_rows, previous_keys, previous_values, incoming_keys, incoming_values, lengths):
    steps, count_of_rows = (query_rows.shape[0], query_rows.shape[1])
    groups = QUERY_HEADS // KEY_VALUE_HEADS
    context_window = previous_keys.shape[1]
    grouped_heads = (
        query_rows.reshape(steps, count_of_rows, KEY_VALUE_HEADS, groups, HEAD_FEATURES)
        .transpose(1, 2, 0, 3, 4)
        .reshape(count_of_rows, KEY_VALUE_HEADS, steps * groups, HEAD_FEATURES)
    )
    keys_previous = previous_keys.reshape(
        count_of_rows, context_window, KEY_VALUE_HEADS, HEAD_FEATURES
    )
    values_previous = previous_values.reshape(
        count_of_rows, context_window, KEY_VALUE_HEADS, HEAD_FEATURES
    )
    keys_incoming = incoming_keys.reshape(
        steps, count_of_rows, KEY_VALUE_HEADS, HEAD_FEATURES
    ).transpose(1, 0, 2, 3)
    values_incoming = incoming_values.reshape(
        steps, count_of_rows, KEY_VALUE_HEADS, HEAD_FEATURES
    ).transpose(1, 0, 2, 3)
    factor = HEAD_FEATURES ** (-0.5)
    score_old = (
        jnp.einsum(
            "rhqd,rchd->rhqc", grouped_heads, keys_previous, preferred_element_type=jnp.float32
        )
        * factor
    )
    score_new = (
        jnp.einsum(
            "rhqd,rshd->rhqs", grouped_heads, keys_incoming, preferred_element_type=jnp.float32
        )
        * factor
    )
    live_old = (jnp.arange(context_window, dtype=jnp.int32)[None, :] < lengths[:, None])[
        :, None, None, :
    ]
    query_step = jnp.arange(steps * groups, dtype=jnp.int32) // groups
    live_new = (jnp.arange(steps, dtype=jnp.int32)[None, :] <= query_step[:, None])[
        None, None, :, :
    ]
    score_old = jnp.where(live_old, score_old, -1e30)
    score_new = jnp.where(live_new, score_new, -1e30)
    peak_score = jnp.maximum(jnp.max(score_old, axis=-1), jnp.max(score_new, axis=-1))
    weight_old = jnp.where(live_old, jnp.exp(score_old - peak_score[..., None]), 0.0)
    weight_new = jnp.where(live_new, jnp.exp(score_new - peak_score[..., None]), 0.0)
    weight_sum = jnp.sum(weight_old, axis=-1) + jnp.sum(weight_new, axis=-1)
    mixed_out = jnp.einsum(
        "rhqc,rchd->rhqd",
        weight_old.astype(jnp.bfloat16),
        values_previous,
        preferred_element_type=jnp.float32,
    )
    mixed_out = mixed_out + jnp.einsum(
        "rhqs,rshd->rhqd",
        weight_new.astype(jnp.bfloat16),
        values_incoming,
        preferred_element_type=jnp.float32,
    )
    mixed_out = (mixed_out / weight_sum[..., None]).astype(jnp.bfloat16)
    return (
        mixed_out.reshape(count_of_rows, KEY_VALUE_HEADS, steps, groups, HEAD_FEATURES)
        .transpose(2, 0, 1, 3, 4)
        .reshape(steps, count_of_rows, -1)
    )


def local(
    inputs,
    norm_gain,
    query_weight,
    key_weight,
    value_weight,
    output_weight,
    query_down,
    query_up,
    output_down,
    output_up,
    block_adapter,
    cache_lengths,
    cache_keys,
    cache_values,
):
    across_first = lax.axis_size("gx")
    across_second = lax.axis_size("gy")
    index_first = lax.axis_index("gx")
    index_second = lax.axis_index("gy")
    steps = inputs.shape[0]
    request_count = inputs.shape[1] * across_second
    width = inputs.shape[2] * across_first
    local_rows = cache_keys.shape[0]
    block_count = block_adapter.shape[0]
    block_rows = request_count // block_count
    query_width = query_weight.shape[1]
    key_width = key_weight.shape[1]
    norm_scale = norm_gain.astype(jnp.float32)
    query_first = pick_adapters(query_down, block_adapter, index_second)
    query_second = pick_adapters(query_up, block_adapter, index_first)
    output_first = pick_adapters(output_down, block_adapter, index_first)
    output_second = pick_adapters(output_up, block_adapter, index_second)
    rows_all = lax.all_gather(inputs, "gy", axis=1, tiled=True)
    rows_wide = rows_all.astype(jnp.float32)
    squares = lax.psum(jnp.sum(rows_wide * rows_wide, axis=2), "gx")
    factor_rows = lax.rsqrt(squares / width + EPS)
    normed = (rows_wide * factor_rows[..., None] * norm_scale).astype(jnp.bfloat16)
    blocked = normed.reshape(steps, block_count, block_rows, -1)
    rank_part = jnp.einsum(
        "tbnd,bdr->tbnr", blocked, query_first, preferred_element_type=jnp.float32
    )
    rank_query = lax.psum(rank_part, ("gx", "gy")).astype(jnp.bfloat16)
    delta_query = jnp.einsum(
        "tbnr,bre->tbne", rank_query, query_second, preferred_element_type=jnp.float32
    ).reshape(steps, request_count, -1)
    part_query = (
        jnp.einsum("tnd,de->tne", normed, query_weight, preferred_element_type=jnp.float32)
        + delta_query
    )
    part_key = jnp.einsum("tnd,de->tne", normed, key_weight, preferred_element_type=jnp.float32)
    part_value = jnp.einsum("tnd,de->tne", normed, value_weight, preferred_element_type=jnp.float32)
    joined = jnp.concatenate([part_query, part_key, part_value], axis=-1)
    summed = lax.psum_scatter(joined, "gx", scatter_dimension=1, tiled=True).astype(jnp.bfloat16)
    chunk_rows = summed.shape[1] // across_second
    spread = lax.all_to_all(
        summed.reshape(steps, across_second, chunk_rows, -1), "gy", 1, 2, tiled=False
    )
    query_full = spread[..., :query_width].reshape(steps, local_rows, -1)
    key_full = spread[..., query_width : query_width + key_width].reshape(steps, local_rows, -1)
    value_full = spread[..., query_width + key_width :].reshape(steps, local_rows, -1)
    token_positions = (
        cache_lengths[None, :] + jnp.arange(steps, dtype=jnp.int32)[:, None]
    ).reshape(-1)
    query_rot = rotary_embedding(
        query_full.astype(jnp.float32).reshape(steps * local_rows, QUERY_HEADS, HEAD_FEATURES),
        token_positions,
    ).astype(jnp.bfloat16)
    key_rot = rotary_embedding(
        key_full.astype(jnp.float32).reshape(steps * local_rows, KEY_VALUE_HEADS, HEAD_FEATURES),
        token_positions,
    ).astype(jnp.bfloat16)
    mixed_local = attend(
        query_rot.reshape(steps, local_rows, -1),
        cache_keys,
        cache_values,
        key_rot.reshape(steps, local_rows, -1),
        value_full,
        cache_lengths,
    )
    head_group = lax.all_to_all(
        mixed_local.reshape(steps, local_rows, across_second, -1), "gy", 2, 1, tiled=False
    ).reshape(steps, across_second * local_rows, -1)
    mixed_all = lax.all_gather(head_group, "gx", axis=1, tiled=True)
    rank_part_out = jnp.einsum(
        "tbnq,bqr->tbnr",
        mixed_all.reshape(steps, block_count, block_rows, -1),
        output_first,
        preferred_element_type=jnp.float32,
    )
    rank_output = lax.psum(rank_part_out, ("gx", "gy")).astype(jnp.bfloat16)
    delta_output = jnp.einsum(
        "tbnr,bre->tbne", rank_output, output_second, preferred_element_type=jnp.float32
    ).reshape(steps, request_count, -1)
    partial_out = (
        jnp.einsum("tnq,qe->tne", mixed_all, output_weight, preferred_element_type=jnp.float32)
        + delta_output
    )
    return lax.psum_scatter(partial_out, "gy", scatter_dimension=1, tiled=True).astype(jnp.bfloat16)


def solution(mesh):
    in_specs = (
        P(None, "gy", "gx"),
        P("gx"),
        P("gx", "gy"),
        P("gx", "gy"),
        P("gx", "gy"),
        P("gy", "gx"),
        P("gy", "gx", None),
        P("gx", None, "gy"),
        P("gx", "gy", None),
        P("gy", None, "gx"),
        P(),
        P(("gx", "gy")),
        P(("gx", "gy"), None, None),
        P(("gx", "gy"), None, None),
    )
    out_specs = P(None, "gy", "gx")
    return jax.shard_map(local, mesh=mesh, in_specs=in_specs, out_specs=out_specs, check_vma=False)
```

profile of v0, /device:TPU:0, one launch (start us, length us, event | category | flops | bytes accessed | tf_op | source)
XLA Modules:
  0.0 441.3 jit_solution(3828490205044012605)
XLA Ops:
  6.5 0.7 all-gather.3.cloned.1.call-update
  7.3 0.0 reduce-scatter.3.cloned.1.call-start
  7.3 1.4 fusion.85
  13.9 0.7 convert_element_type.60
  14.6 1.0 dynamic-slice_select_fusion.7
  15.6 1.1 dynamic-slice_select_fusion.3
  16.7 14.6 %all-gather.3.cloned.1.call-done = bf16[3,256,1024]{2,1,0:T(8,128)(2,1)} async-done(((bf16[3,64,1024]{2,1,0:T(8,128)(2,1)}), bf16[3,256,1024]{2,1,0:T(8,128)(2,1)}) %all-gather.3.cloned.1.call-update) | async-done | bytes 1572880 | tf_op jit(solution)/shard_map/all_gather | solution.py:139
  31.3 1.8 fusion.12
  33.1 21.4 %psum.21 = f32[3,256]{1,0:T(4,128)S(1)} all-reduce(f32[3,256]{1,0:T(4,128)S(1)} %fusion.12), channel_id=1, replica_groups=mesh['gx'=8,'gy'=4] {'gx'}, use_global_device_ids=true, to_apply=%region_1.2 | all-reduce | flops 768 | bytes 6144 | tf_op jit(solution)/shard_map/psum | solution.py:141
  54.5 1.8 fusion.14
  56.3 0.6 fusion.28
  56.9 39.3 %all-reduce.2 = bf16[3,2,128,64]{2,3,0,1:T(8,128)(2,1)S(1)} all-reduce(f32[3,2,128,64]{2,3,0,1:T(8,128)S(1)} %fusion.28), channel_id=1, replica_groups=mesh['gx'=8,'gy'=4] {'gx','gy'}, use_global_device_ids=true, to_apply=%region_2.3 | all-reduce | flops 49152 | bytes 294912 | tf_op jit(solution)/shard_map/psum | solution.py:148
  96.2 1.0 convolution_bitcast_fusion
  97.3 0.0 copy-start.2
  97.3 0.8 copy.39
  98.1 0.0 copy-start.4
  98.1 0.6 fusion.52
  98.7 0.6 fusion.54
  99.3 1.0 copy-done.4
  100.3 3.5 bitcast_add_fusion
  103.8 3.5 pad_maximum_fusion
  107.3 0.0 reduce-scatter.3.cloned.1.call-update
  107.4 0.6 copy-done.3
  108.0 0.1 iota_compare_fusion
  108.1 139.1 %reduce-scatter.3.cloned.1.call-done = f32[3,32,2560]{2,1,0:T(8,128)} async-done(((f32[3,256,2560]{2,1,0:T(8,128)}), f32[3,32,2560]{2,1,0:T(8,128)}) %reduce-scatter.3.cloned.1.call-update) | async-done | bytes 983056 | tf_op jit(solution)/shard_map/reduce_scatter | solution.py:159
  247.1 1.3 convert_bitcast_fusion
  248.4 0.8 copy.44
  249.2 3.5 all-to-all-start
  252.7 0.2 all-gather.5.cloned.1.call-start
  252.9 0.1 convert_element_type.67
  253.0 0.1 multiply_cosine_fusion
  253.1 8.0 %all-to-all-done = bf16[3,4,8,1,2560]{4,2,0,3,1:T(8,128)(2,1)S(1)} async-done(((bf16[3,4,8,1,2560]{4,2,0,3,1:T(8,128)(2,1)}), bf16[3,4,8,1,2560]{4,2,0,3,1:T(8,128)(2,1)S(1)}, u32[]{:S(2)}, u32[]{:S(2)}) %all-to-all-start) | async-done | bytes 491552 | tf_op jit(solution)/shard_map/all_to_all | solution.py:161
  261.1 0.1 slice_convert_fusion
  261.2 0.5 copy.45
  261.7 0.4 reshape.182
  262.3 0.4 subtract_convert_fusion
  262.6 0.1 subtract_convert_fusion.1
  262.8 4.6 %fusion.86 = (f32[8,8,24]{2,1,0:T(8,128)S(1)}, f32[8,8,24,256]{3,2,1,0:T(8,128)S(1)}) fusion(pred[8,256]{1,0:T(8,128)(4,1)S(1)} %iota_compare_fusion, bf16[8,256,1024]{2,1,0:T(8,128)(2,1)} %param.26, bf16[3,8,8,8,64]{4,3,2,1,0:T(8,128)(2,1)S(1)} %bitcast.137, bf16[3,8,8,8,64]{4,3,2,1,0:T(8,128)(2,1)S(1)} %bitcast.135), kind=kOutput, calls=%fused_computation.111 | convolution fusion | flops 102627840 | bytes 6168576 | tf_op jit(solution)/shard_map/rhqd,rchd->rhqc/dot_general | solution.py:62
  267.4 0.4 fusion.87
  267.9 0.1 fusion.66
  268.0 0.6 fusion.26
  268.6 0.4 fusion.68
  269.1 3.1 fusion.41
  272.2 0.1 copy.117
  272.3 0.1 broadcast_in_dim_reshape_reshape.3
  272.4 0.2 copy.55
  272.6 9.8 %all_to_all.30 = bf16[3,1,8,4,2048]{4,2,0,1,3:T(8,128)(2,1)S(1)} all-to-all(bf16[3,1,8,4,2048]{4,2,0,1,3:T(8,128)(2,1)S(1)} %copy.55), channel_id=1, replica_groups=mesh['gx'=8,'gy'=4] {'gy'}, dimensions={3} | all-to-all | bytes 786432 | tf_op jit(solution)/shard_map/all_to_all | solution.py:186
  282.4 0.8 copy_bitcast_fusion
  283.2 0.0 all-gather.5.cloned.1.call-update
  283.2 0.0 reduce-scatter.5.cloned.1.call-start
  283.3 1.0 dynamic-slice_select_fusion.5
  284.3 1.1 dynamic-slice_select_fusion.1
  285.4 56.7 %all-gather.5.cloned.1.call-done = bf16[3,256,2048]{2,1,0:T(8,128)(2,1)} async-done(((bf16[3,32,2048]{2,1,0:T(8,128)(2,1)}), bf16[3,256,2048]{2,1,0:T(8,128)(2,1)}) %all-gather.5.cloned.1.call-update) | async-done | bytes 3145744 | tf_op jit(solution)/shard_map/all_gather | solution.py:189
  342.1 3.0 fusion.31
  345.1 42.6 %all-reduce.3 = bf16[3,2,128,64]{2,3,0,1:T(8,128)(2,1)S(1)} all-reduce(f32[3,2,128,64]{2,3,0,1:T(8,128)S(1)} %fusion.31), channel_id=1, replica_groups=mesh['gx'=8,'gy'=4] {'gx','gy'}, use_global_device_ids=true, to_apply=%region_8.9 | all-reduce | flops 49152 | bytes 294912 | tf_op jit(solution)/shard_map/psum | solution.py:196
  387.7 0.6 convolution_bitcast_fusion.1
  388.3 0.0 copy-start.5
  388.3 0.4 copy.58
  388.7 0.9 copy-done.6
  389.5 1.4 copy-done.5
  390.9 5.1 %bitcast_add_fusion.1 = f32[3,256,1024]{2,1,0:T(8,128)} fusion(f32[3,2,128,1024]{3,2,1,0:T(8,128)S(1)} %copy.58, bf16[3,256,2048]{2,1,0:T(8,128)(2,1)S(1)} %copy-done.6, bf16[2048,1024]{1,0:T(8,128)(2,1)S(1)} %copy-done.5), kind=kOutput, calls=%fused_computation.18 | convolution fusion | flops 3222011904 | bytes 13631488 | tf_op jit(solution)/shard_map/tnq,qe->tne/dot_general | solution.py:201
  396.0 0.0 reduce-scatter.5.cloned.1.call-update
  396.1 36.8 %reduce-scatter.5.cloned.1.call-done = f32[3,64,1024]{2,1,0:T(8,128)} async-done(((f32[3,256,1024]{2,1,0:T(8,128)}), f32[3,64,1024]{2,1,0:T(8,128)}) %reduce-scatter.5.cloned.1.call-update) | async-done | bytes 786448 | tf_op jit(solution)/shard_map/reduce_scatter | solution.py:204
  432.8 1.9 convert_element_type.74
  (22 shorter events, 0.3 us)
Async XLA Ops:
  6.5 91.5 %copy-start = (bf16[1024,256]{1,0:T(8,128)(2,1)S(1)}, bf16[1024,256]{1,0:T(8,128)(2,1)}, u32[]{:S(2)}) copy-start(bf16[1024,256]{1,0:T(8,128)(2,1)} %param.18) | copy-start | bytes 1572868
  6.5 24.8 %all-gather.3.cloned.1.call-start = ((), (), s32[]{:S(2)}) async-start(), calls=%async_computation.4 | async-start | bytes 1966080 | tf_op jit(solution)/shard_map/all_gather | solution.py:139
  7.3 239.9 %reduce-scatter.3.cloned.1.call-start = ((), (), s32[]{:S(2)}) async-start(), calls=%async_computation.5 | async-start | bytes 8847360 | tf_op jit(solution)/shard_map/reduce_scatter | solution.py:159
  97.3 1.4 copy-start.2
  98.1 2.2 copy-start.4
  107.3 0.7 copy-start.3
  249.2 11.9 %all-to-all-start = ((bf16[3,4,8,1,2560]{4,2,0,3,1:T(8,128)(2,1)}), bf16[3,4,8,1,2560]{4,2,0,3,1:T(8,128)(2,1)S(1)}, u32[]{:S(2)}, u32[]{:S(2)}) async-start(bf16[3,4,8,1,2560]{4,2,0,3,1:T(8,128)(2,1)} %copy.44), calls=%async_computation.1 | async-start | bytes 983040 | tf_op jit(solution)/shard_map/all_to_all | solution.py:161
  252.7 89.4 %all-gather.5.cloned.1.call-start = ((), (), s32[]{:S(2)}) async-start(), calls=%async_computation.6 | async-start | bytes 3538944 | tf_op jit(solution)/shard_map/all_gather | solution.py:189
  283.2 149.6 %reduce-scatter.5.cloned.1.call-start = ((), (), s32[]{:S(2)}) async-start(), calls=%async_computation.7 | async-start | bytes 3932160 | tf_op jit(solution)/shard_map/reduce_scatter | solution.py:204
  387.6 1.9 copy-start.6
  388.3 2.7 copy-start.5
  390.9 43.8 %copy-start.1 = (bf16[1024,256]{1,0:T(8,128)(2,1)S(1)}, bf16[1024,256]{1,0:T(8,128)(2,1)}, u32[]{:S(2)}) copy-start(bf16[1024,256]{1,0:T(8,128)(2,1)} %param.18) | copy-start | bytes 1572868
Sparse Core Ops, SparseCore 0:
  8.9 22.3 all-gather.2
  107.5 139.6 reduce-scatter.2
  283.4 58.6 all-gather.4
  396.2 36.6 reduce-scatter.4
where the time goes:
time: 442 us; the launch traced here: 441 us
  waiting for transfers between devices  256 us (58%)
  blocking collectives  113 us (26%)
  matrix products  23.5 us (5%)
  between operations  18.7 us (4%)
  other arithmetic  16.6 us (4%)
  local copies, waits for them, and re-layouts  9.71 us (2%)
    reduce_scatter x1, waiting for transfers between devices, local(): lax.psum_scatter(joined, 'gx', scatter_dimension=1, tiled=True)  139 us
    all_gather x1, waiting for transfers between devices, local(): mixed_all = lax.all_gather(head_group, 'gx', axis=1, tiled=True)  56.7 us
    psum x1, blocking collectives, local(): rank_output = lax.psum(rank_part_out, ('gx', 'gy')).astype(jnp.bfloat16)  42.6 us
    psum x1, blocking collectives, local(): rank_query = lax.psum(rank_part, ('gx', 'gy')).astype(jnp.bfloat16)  39.3 us
    reduce_scatter x1, waiting for transfers between devices, local(): lax.psum_scatter(partial_out, 'gy', scatter_dimension=1, tiled=True)  36.8 us
    psum x1, blocking collectives, local(): squares = lax.psum(jnp.sum(rows_wide * rows_wide, axis=2), 'gx')  21.4 us
    all_gather x1, waiting for transfers between devices, local(): rows_all = lax.all_gather(inputs, 'gy', axis=1, tiled=True)  14.6 us
    all_to_all x1, blocking collectives, local(): lax.all_to_all(mixed_local.reshape(steps, local_rows, across_second, -1),...  9.84 us
  transfers between devices with their start and end apart: 5, of which 5 were waited for; matrix products, arithmetic and copies ran while one was open for 1% of the time, Pallas kernels for 0%

commit v1 on v0

--- a/solution.py
+++ b/solution.py
@@ -145,7 +145,7 @@
     rank_part = jnp.einsum(
         "tbnd,bdr->tbnr", blocked, query_first, preferred_element_type=jnp.float32
     )
-    rank_query = lax.psum(rank_part, ("gx", "gy")).astype(jnp.bfloat16)
+    rank_query = jax.lax.psum(jax.lax.psum(rank_part, "gy"), "gx").astype(jnp.bfloat16)
     delta_query = jnp.einsum(
         "tbnr,bre->tbne", rank_query, query_second, preferred_element_type=jnp.float32
     ).reshape(steps, request_count, -1)

time: 442 us -> 467 us (1.057)
  waiting for transfers between devices: 256 us -> 278 us
    psum x0 -> x1, waiting for transfers between devices: none -> 25 us  [local(): jax.lax.psum(rank_part, 'gy')]
  transfers between devices with their start and end apart: 5 -> 6, of which waited for: 5 -> 6; matrix products, arithmetic and copies ran while one was open for 1% -> 2% of each run, Pallas kernels for 0% -> 0%
where the time goes in v1:
time: 467 us; the launch traced here: 466 us
  waiting for transfers between devices  278 us (60%)
  blocking collectives  113 us (24%)
  matrix products  26.1 us (6%)
  between operations  18.7 us (4%)
  other arithmetic  16.6 us (4%)
  local copies, waits for them, and re-layouts  10.1 us (2%)
    reduce_scatter x1, waiting for transfers between devices, local(): lax.psum_scatter(joined, 'gx', scatter_dimension=1, tiled=True)  136 us
    all_gather x1, waiting for transfers between devices, local(): mixed_all = lax.all_gather(head_group, 'gx', axis=1, tiled=True)  56.8 us
    psum x1, blocking collectives, local(): rank_output = lax.psum(rank_part_out, ('gx', 'gy')).astype(jnp.bfloat16)  42.6 us
    psum x1, blocking collectives, local(): jax.lax.psum(jax.lax.psum(rank_part, 'gy'), 'gx').astype(jnp.bfloat16)  39.7 us
    reduce_scatter x1, waiting for transfers between devices, local(): lax.psum_scatter(partial_out, 'gy', scatter_dimension=1, tiled=True)  36.8 us
    psum x1, waiting for transfers between devices, local(): jax.lax.psum(rank_part, 'gy')  25 us
    psum x1, blocking collectives, local(): squares = lax.psum(jnp.sum(rows_wide * rows_wide, axis=2), 'gx')  21.4 us
    all_gather x1, waiting for transfers between devices, local(): rows_all = lax.all_gather(inputs, 'gy', axis=1, tiled=True)  14.6 us
  transfers between devices with their start and end apart: 6, of which 6 were waited for; matrix products, arithmetic and copies ran while one was open for 2% of the time, Pallas kernels for 0%

profile of v1, /device:TPU:0, one launch (start us, length us, event | category | flops | bytes accessed | tf_op | source)
XLA Modules:
  0.0 466.3 jit_solution(8800747580481724320)
XLA Ops:
  6.5 0.7 all-gather.3.cloned.1.call-update
  7.3 0.0 all-reduce.4.cloned.1.call-start
  7.3 1.4 fusion.85
  13.9 0.7 convert_element_type.60
  14.6 1.0 dynamic-slice_select_fusion.7
  15.6 1.1 dynamic-slice_select_fusion.3
  16.7 14.6 %all-gather.3.cloned.1.call-done = bf16[3,256,1024]{2,1,0:T(8,128)(2,1)} async-done(((bf16[3,64,1024]{2,1,0:T(8,128)(2,1)}), bf16[3,256,1024]{2,1,0:T(8,128)(2,1)}) %all-gather.3.cloned.1.call-update) | async-done | bytes 1572880 | tf_op jit(solution)/shard_map/all_gather | solution.py:139
  31.3 1.8 fusion.12
  33.1 21.4 %psum.28 = f32[3,256]{1,0:T(4,128)S(1)} all-reduce(f32[3,256]{1,0:T(4,128)S(1)} %fusion.12), channel_id=1, replica_groups=mesh['gx'=8,'gy'=4] {'gx'}, use_global_device_ids=true, to_apply=%region_1.2 | all-reduce | flops 768 | bytes 6144 | tf_op jit(solution)/shard_map/psum | solution.py:141
  54.5 1.8 fusion.14
  56.3 1.3 fusion.28
  57.6 0.0 all-reduce.4.cloned.1.call-update
  57.6 0.0 reduce-scatter.3.cloned.1.call-start
  57.7 0.6 fusion.52
  58.3 2.5 fusion.54
  60.8 25.0 %all-reduce.4.cloned.1.call-done = f32[3,2,128,64]{2,3,0,1:T(8,128)} async-done(((f32[3,2,128,64]{2,3,0,1:T(8,128)}), f32[3,2,128,64]{2,3,0,1:T(8,128)}) %all-reduce.4.cloned.1.call-update) | async-done | bytes 196624 | tf_op jit(solution)/shard_map/psum | solution.py:148
  85.8 39.7 %all-reduce.5 = bf16[3,2,128,64]{2,3,0,1:T(8,128)(2,1)S(1)} all-reduce(f32[3,2,128,64]{2,3,0,1:T(8,128)} %all-reduce.4.cloned.1.call-done), channel_id=1, replica_groups=mesh['gx'=8,'gy'=4] {'gx'}, use_global_device_ids=true, to_apply=%region_3.4 | all-reduce | flops 49152 | bytes 294912 | tf_op jit(solution)/shard_map/psum | solution.py:148
  125.5 1.0 convolution_bitcast_fusion
  126.5 0.8 copy.39
  127.3 1.4 copy-done.4
  128.7 3.5 bitcast_add_fusion
  132.2 3.5 pad_maximum_fusion
  135.7 0.0 reduce-scatter.3.cloned.1.call-update
  135.7 0.6 copy-done.3
  136.4 0.1 iota_compare_fusion
  136.4 135.7 %reduce-scatter.3.cloned.1.call-done = f32[3,32,2560]{2,1,0:T(8,128)} async-done(((f32[3,256,2560]{2,1,0:T(8,128)}), f32[3,32,2560]{2,1,0:T(8,128)}) %reduce-scatter.3.cloned.1.call-update) | async-done | bytes 983056 | tf_op jit(solution)/shard_map/reduce_scatter | solution.py:159
  272.1 1.3 convert_bitcast_fusion
  273.4 0.8 copy.44
  274.2 3.5 all-to-all-start
  277.7 0.2 all-gather.5.cloned.1.call-start
  277.9 0.1 convert_element_type.67
  278.0 0.1 multiply_cosine_fusion
  278.1 8.0 %all-to-all-done = bf16[3,4,8,1,2560]{4,2,0,3,1:T(8,128)(2,1)S(1)} async-done(((bf16[3,4,8,1,2560]{4,2,0,3,1:T(8,128)(2,1)}), bf16[3,4,8,1,2560]{4,2,0,3,1:T(8,128)(2,1)S(1)}, u32[]{:S(2)}, u32[]{:S(2)}) %all-to-all-start) | async-done | bytes 491552 | tf_op jit(solution)/shard_map/all_to_all | solution.py:161
  286.1 0.1 slice_convert_fusion
  286.2 0.5 copy.45
  286.7 0.4 reshape.182
  287.2 0.4 subtract_convert_fusion
  287.6 0.1 subtract_convert_fusion.1
  287.8 4.6 fusion.86
  292.4 0.4 fusion.87
  292.9 0.1 fusion.66
  293.0 0.6 fusion.26
  293.6 0.4 fusion.68
  294.1 3.1 fusion.41
  297.2 0.1 copy.117
  297.3 0.1 broadcast_in_dim_reshape_reshape.3
  297.4 0.2 copy.55
  297.6 9.8 %all_to_all.30 = bf16[3,1,8,4,2048]{4,2,0,1,3:T(8,128)(2,1)S(1)} all-to-all(bf16[3,1,8,4,2048]{4,2,0,1,3:T(8,128)(2,1)S(1)} %copy.55), channel_id=1, replica_groups=mesh['gx'=8,'gy'=4] {'gy'}, dimensions={3} | all-to-all | bytes 786432 | tf_op jit(solution)/shard_map/all_to_all | solution.py:186
  307.4 0.8 copy_bitcast_fusion
  308.2 0.0 all-gather.5.cloned.1.call-update
  308.2 0.0 reduce-scatter.5.cloned.1.call-start
  308.3 1.0 dynamic-slice_select_fusion.5
  309.3 1.1 dynamic-slice_select_fusion.1
  310.4 56.8 %all-gather.5.cloned.1.call-done = bf16[3,256,2048]{2,1,0:T(8,128)(2,1)} async-done(((bf16[3,32,2048]{2,1,0:T(8,128)(2,1)}), bf16[3,256,2048]{2,1,0:T(8,128)(2,1)}) %all-gather.5.cloned.1.call-update) | async-done | bytes 3145744 | tf_op jit(solution)/shard_map/all_gather | solution.py:189
  367.1 3.0 fusion.31
  370.1 42.6 %all-reduce.6 = bf16[3,2,128,64]{2,3,0,1:T(8,128)(2,1)S(1)} all-reduce(f32[3,2,128,64]{2,3,0,1:T(8,128)S(1)} %fusion.31), channel_id=1, replica_groups=mesh['gx'=8,'gy'=4] {'gx','gy'}, use_global_device_ids=true, to_apply=%region_9.10 | all-reduce | flops 49152 | bytes 294912 | tf_op jit(solution)/shard_map/psum | solution.py:196
  412.7 0.6 convolution_bitcast_fusion.1
  413.3 0.4 copy.58
  413.7 0.9 copy-done.6
  414.6 1.4 copy-done.5
  416.0 5.1 %bitcast_add_fusion.1 = f32[3,256,1024]{2,1,0:T(8,128)} fusion(f32[3,2,128,1024]{3,2,1,0:T(8,128)S(1)} %copy.58, bf16[3,256,2048]{2,1,0:T(8,128)(2,1)S(1)} %copy-done.6, bf16[2048,1024]{1,0:T(8,128)(2,1)S(1)} %copy-done.5), kind=kOutput, calls=%fused_computation.18 | convolution fusion | flops 3222011904 | bytes 13631488 | tf_op jit(solution)/shard_map/tnq,qe->tne/dot_general | solution.py:201
  421.1 0.0 reduce-scatter.5.cloned.1.call-update
  421.1 36.8 %reduce-scatter.5.cloned.1.call-done = f32[3,64,1024]{2,1,0:T(8,128)} async-done(((f32[3,256,1024]{2,1,0:T(8,128)}), f32[3,64,1024]{2,1,0:T(8,128)}) %reduce-scatter.5.cloned.1.call-update) | async-done | bytes 786448 | tf_op jit(solution)/shard_map/reduce_scatter | solution.py:204
  457.8 1.9 convert_element_type.74
  (25 shorter events, 0.3 us)
Async XLA Ops:
  6.5 51.1 %copy-start = (bf16[1024,256]{1,0:T(8,128)(2,1)S(1)}, bf16[1024,256]{1,0:T(8,128)(2,1)}, u32[]{:S(2)}) copy-start(bf16[1024,256]{1,0:T(8,128)(2,1)} %param.18) | copy-start | bytes 1572868
  6.5 24.8 %all-gather.3.cloned.1.call-start = ((), (), s32[]{:S(2)}) async-start(), calls=%async_computation.4 | async-start | bytes 1966080 | tf_op jit(solution)/shard_map/all_gather | solution.py:139
  7.3 78.5 %all-reduce.4.cloned.1.call-start = ((), (), s32[]{:S(2)}) async-start(), calls=%async_computation.5 | async-start | bytes 393216 | tf_op jit(solution)/shard_map/psum | solution.py:148
  57.6 214.5 %reduce-scatter.3.cloned.1.call-start = ((), (), s32[]{:S(2)}) async-start(), calls=%async_computation.6 | async-start | bytes 8847360 | tf_op jit(solution)/shard_map/reduce_scatter | solution.py:159
  126.5 2.2 copy-start.4
  128.7 3.5 copy-start.2
  135.7 0.7 copy-start.3
  274.2 11.9 %all-to-all-start = ((bf16[3,4,8,1,2560]{4,2,0,3,1:T(8,128)(2,1)}), bf16[3,4,8,1,2560]{4,2,0,3,1:T(8,128)(2,1)S(1)}, u32[]{:S(2)}, u32[]{:S(2)}) async-start(bf16[3,4,8,1,2560]{4,2,0,3,1:T(8,128)(2,1)} %copy.44), calls=%async_computation.1 | async-start | bytes 983040 | tf_op jit(solution)/shard_map/all_to_all | solution.py:161
  277.7 89.5 %all-gather.5.cloned.1.call-start = ((), (), s32[]{:S(2)}) async-start(), calls=%async_computation.7 | async-start | bytes 3538944 | tf_op jit(solution)/shard_map/all_gather | solution.py:189
  308.2 149.6 %reduce-scatter.5.cloned.1.call-start = ((), (), s32[]{:S(2)}) async-start(), calls=%async_computation.8 | async-start | bytes 3932160 | tf_op jit(solution)/shard_map/reduce_scatter | solution.py:204
  412.7 1.9 copy-start.6
  413.3 2.7 copy-start.5
  416.0 43.8 %copy-start.1 = (bf16[1024,256]{1,0:T(8,128)(2,1)S(1)}, bf16[1024,256]{1,0:T(8,128)(2,1)}, u32[]{:S(2)}) copy-start(bf16[1024,256]{1,0:T(8,128)(2,1)} %param.18) | copy-start | bytes 1572868
Sparse Core Ops, SparseCore 0:
  8.9 22.3 all-gather.2
  57.7 28.0 all-reduce.3
  135.9 136.2 reduce-scatter.2
  308.4 58.7 all-gather.4
  421.2 36.5 reduce-scatter.4
